TPU v7x, 256 devices: a whole 4x4x8 slice. The times are simulated.
256 devices in a mesh: section: 8 (over x, core), dp: 32 (over y, z).
Axes of the slice: x: 4, y: 4, z: 8, core: 2. Of those that a mesh axis runs over, the one named last changes fastest.
Arguments:
- resid_in: bfloat16 [4, 1024, 2048], P(None, 'dp'), may hold values from -10 to 10
- dest_row: int32 [4, 1024], replicated, may hold values from 0 to 1023, as said below
- doc_ids: int32 [4, 1024], P(None, 'dp'), may hold values from 0 to 1023, as said below
- cotangent: bfloat16 [4, 1024, 2048], P(None, 'dp'), may hold values from -0.119628906 to 0.119628906
- gain: float32 [8, 2048], P('section'), may hold values from 0.5 to 1.5
- steer: float32 [8, 2048], P('section'), may hold values from -3 to 3
- w_query: bfloat16 [8, 2048, 1024], P('section', 'dp'), may hold values from -1 to 1
- w_keyval: bfloat16 [8, 2048, 512], P('section', 'dp'), may hold values from -1 to 1
- w_out: bfloat16 [8, 1024, 2048], P('section', None, 'dp'), may hold values from -0.1875 to 0.1875
Outputs:
- hidden_out: bfloat16 [8, 4, 1024, 2048], P('section', None, 'dp')
- grad_steer: float32 [8, 2048], P('section')
Inputs may be any that keep to these rules, and one draw needn't show every extreme that they name: Each row of dest_row is a permutation of 0 to 1023. Counting the tokens of one aligned block of 32 input tokens that go to one aligned block of 32 packed rows, no count exceeds 2, and some reach it in every micro-batch. doc_ids never falls along a row; every value is a row index r at which doc_ids equals r; each aligned block of 32 rows begins a document, so no document crosses such a block.
All inputs are finite; a program needn't handle non-finite values.
Results may differ from a plain program's by a relative error of at most 0.02.
Values may be sent and summed in bfloat16 or wider, within the bound.
No kernel may reach another device: no remote copies, remote signals or barrier semaphores. Data moves between devices by JAX's collectives and lax.ppermute only.
A program may use at most 64 MiB of HBM per device.

v0:
```python
import jax
import jax.numpy as jnp
from jax import lax
from jax.sharding import PartitionSpec as P

HD = 64
ROPE_BASE = 500000.0
EPSILON = 1e-05
MASKED = -1e30


def rope_tables(positions):
    half_size = HD // 2
    freq_index = jnp.arange(half_size, dtype=jnp.float32)
    inverse = ROPE_BASE ** (-2.0 * freq_index / HD)
    angles = positions.astype(jnp.float32)[..., None] * inverse
    return (jnp.cos(angles)[..., None, :], jnp.sin(angles)[..., None, :])


def rotate(values, tables):
    half_size = values.shape[-1] // 2
    cosine, sine_part = tables
    first_half = values[..., :half_size]
    second = values[..., half_size:]
    return jnp.concatenate(
        [first_half * cosine - second * sine_part, second * cosine + first_half * sine_part],
        axis=-1,
    )


def normalize(hidden_in, steering, gain_row):
    residual = hidden_in.astype(jnp.float32) + steering
    normed = (
        residual
        * lax.rsqrt(jnp.mean(residual * residual, axis=-1, keepdims=True) + EPSILON)
        * gain_row
    ).astype(jnp.bfloat16)
    return (residual, normed)


def attend(projected_in, tables, allowed, query_heads):
    row_count = projected_in.shape[0]
    head_size = HD
    query_cols = query_heads * head_size
    kv_heads = (projected_in.shape[1] - query_cols) // (2 * head_size)
    group_size = query_heads // kv_heads
    queries = projected_in[:, :query_cols].reshape(row_count, query_heads, head_size)
    keyval = projected_in[:, query_cols:]
    key_rows = rotate(
        keyval[:, : kv_heads * head_size].reshape(row_count, kv_heads, head_size), tables
    ).astype(jnp.bfloat16)
    values = (
        keyval[:, kv_heads * head_size :]
        .reshape(row_count, kv_heads, head_size)
        .astype(jnp.bfloat16)
    )
    queries = (
        rotate(queries, tables)
        .astype(jnp.bfloat16)
        .reshape(row_count, kv_heads, group_size, head_size)
    )
    scores = jnp.einsum(
        "rkgd,skd->kgrs", queries, key_rows, preferred_element_type=jnp.float32
    ) * head_size ** (-0.5)
    scores = jnp.where(allowed[None, None], scores, MASKED)
    peak = jnp.max(scores, axis=-1, keepdims=True)
    weights = jnp.exp(scores - peak)
    weights = (weights / jnp.sum(weights, axis=-1, keepdims=True)).astype(jnp.bfloat16)
    mixed_heads = jnp.einsum(
        "kgrs,skd->rkgd", weights, values, preferred_element_type=jnp.float32
    ).astype(jnp.bfloat16)
    return mixed_heads.reshape(row_count, query_heads * head_size)


def project_in(normed, w_qkv):
    return jnp.dot(normed, w_qkv, preferred_element_type=jnp.float32)


def project_out(residual, mixed_heads, w_out):
    return (residual + jnp.dot(mixed_heads, w_out, preferred_element_type=jnp.float32)).astype(
        jnp.bfloat16
    )


def layer_forward(hidden_in, steering, gain_row, w_qkv, w_out, tables, allowed):
    residual, normed = normalize(hidden_in, steering, gain_row)
    projected_in = project_in(normed, w_qkv)
    mixed_heads = attend(projected_in, tables, allowed, w_out.shape[0] // HD)
    return (project_out(residual, mixed_heads, w_out), projected_in)


def layer_backward(
    hidden_in, steering, projected_in, upstream, gain_row, w_qkv, w_out, tables, allowed
):
    query_heads = w_out.shape[0] // HD
    (residual, normed), normalize_pull = jax.vjp(
        lambda h, s: normalize(h, s, gain_row), hidden_in, steering
    )
    mixed_heads, attend_pull = jax.vjp(
        lambda p: attend(p, tables, allowed, query_heads), projected_in
    )
    unused_out, out_pull = jax.vjp(lambda r, m: project_out(r, m, w_out), residual, mixed_heads)
    grad_residual, grad_mixed = out_pull(upstream)
    (grad_projected,) = attend_pull(grad_mixed)
    unused_proj, in_pull = jax.vjp(lambda n: project_in(n, w_qkv), normed)
    (grad_normed,) = in_pull(grad_projected)
    return normalize_pull((grad_residual, grad_normed))


def butterfly_sum(values, axis):
    count = lax.axis_size(axis)
    index = lax.axis_index(axis)
    stride = 1
    while stride < count:
        fan = 4 if count % (stride * 4) == 0 else 2
        local = index // stride % fan
        received = [values]
        for offset in range(1, fan):
            route = [
                (
                    i,
                    i // (stride * fan) * stride * fan
                    + (i // stride % fan ^ offset) * stride
                    + i % stride,
                )
                for i in range(count)
            ]
            received.append(lax.ppermute(values, axis, route))
        stacked = jnp.stack(received)
        ordered = [
            lax.dynamic_index_in_dim(stacked, local ^ m, 0, keepdims=False) for m in range(fan)
        ]
        if fan == 4:
            values = ordered[0] + ordered[1] + (ordered[2] + ordered[3])
        else:
            values = ordered[0] + ordered[1]
        stride *= fan
    return values


def plan_slots(target, device, row_count, capacity, dp_count):
    target_grid = target.reshape(dp_count, row_count)
    target_dev = target_grid // row_count
    target_off = target_grid % row_count
    row_order = jnp.arange(row_count, dtype=jnp.int32)
    matching = target_dev[:, :, None] == target_dev[:, None, :]
    earlier = row_order[None, :] < row_order[:, None]
    rank_ids = jnp.sum((matching & earlier[None]).astype(jnp.int32), axis=2)
    slot_ids = target_dev * capacity + rank_ids
    own_slot = lax.dynamic_index_in_dim(slot_ids, device, 0, keepdims=False)
    column_ids = jnp.arange(dp_count, dtype=jnp.int32)[:, None] * capacity + rank_ids
    landing = (target_dev == device)[None] & (target_off[None] == row_order[:, None, None])
    source_col = jnp.sum(jnp.where(landing, column_ids[None], 0), axis=(1, 2))
    return (own_slot, source_col)


def pack_rows(source_rows, own_slot, slot_count):
    selector = (jnp.arange(slot_count, dtype=jnp.int32)[:, None] == own_slot[None, :]).astype(
        jnp.bfloat16
    )
    return jnp.dot(selector, source_rows, preferred_element_type=jnp.float32).astype(jnp.bfloat16)


def unpack_rows(arrived, source_col):
    selector = (
        source_col[:, None] == jnp.arange(arrived.shape[0], dtype=jnp.int32)[None, :]
    ).astype(jnp.bfloat16)
    return jnp.dot(selector, arrived, preferred_element_type=jnp.float32).astype(jnp.bfloat16)


def body(resid_in, dest_row, doc_ids, cotangent, gain, steer, w_query, w_keyval, w_out):
    dp_count = lax.axis_size("dp")
    section_count = lax.axis_size("section")
    device = lax.axis_index("dp")
    section_idx = lax.axis_index("section")
    micro_count, row_count, width = resid_in.shape
    capacity = row_count // dp_count + 1
    slot_count = dp_count * capacity
    full_qkv = lax.all_gather(
        jnp.concatenate([w_query[0], w_keyval[0]], axis=1), "dp", axis=0, tiled=True
    )
    full_out = lax.all_gather(w_out[0], "dp", axis=1, tiled=True)
    gain_row = gain[0]
    steering = steer[0]
    plans = [
        plan_slots(dest_row[micro_idx], device, row_count, capacity, dp_count)
        for micro_idx in range(micro_count)
    ]
    packed = jnp.stack(
        [
            pack_rows(resid_in[micro_idx], plans[micro_idx][0], slot_count).reshape(
                dp_count, capacity, width
            )
            for micro_idx in range(micro_count)
        ],
        axis=1,
    )
    arrived = lax.all_to_all(packed, "dp", split_axis=0, concat_axis=0, tiled=True)
    grouped = jnp.stack(
        [
            unpack_rows(arrived[:, micro_idx].reshape(slot_count, width), plans[micro_idx][1])
            for micro_idx in range(micro_count)
        ]
    )
    global_rows = device * row_count + jnp.arange(row_count, dtype=jnp.int32)
    flat_count = micro_count * row_count
    tables = rope_tables((global_rows[None, :] - doc_ids).reshape(flat_count))
    micro_of = jnp.arange(flat_count, dtype=jnp.int32) // row_count
    doc_keys = doc_ids.reshape(flat_count) + micro_of * (dp_count * row_count)
    flat_index = jnp.arange(flat_count, dtype=jnp.int32)
    allowed = (doc_keys[:, None] == doc_keys[None, :]) & (
        flat_index[:, None] >= flat_index[None, :]
    )
    grouped = grouped.reshape(flat_count, width)
    cotangent = cotangent.reshape(flat_count, width)

    def run_layer(hidden_in, steer_vec):
        return layer_forward(hidden_in, steer_vec, gain_row, full_qkv, full_out, tables, allowed)

    zero_block = jnp.zeros((flat_count, width), jnp.bfloat16)
    zero_proj = jnp.zeros((flat_count, full_qkv.shape[1]), jnp.float32)

    def precompute(hidden_in):
        return project_in(normalize(hidden_in, steering, gain_row)[1], full_qkv)

    forward_route = [(i, i + 1) for i in range(section_count - 1)]
    backward_route = [(i + 1, i) for i in range(section_count - 1)]

    def forward_step(carry, unused):
        hidden_in, kept, produced, step = carry
        active = section_idx == step
        kept = jnp.where(active, hidden_in, kept)
        hidden_new = lax.cond(active, lambda: run_layer(hidden_in, steering)[0], lambda: zero_block)
        produced = jnp.where(active, hidden_new, produced)
        sent = lax.ppermute(hidden_new, "section", forward_route)
        return ((sent, kept, produced, step + 1), None)

    (unused_in, kept, produced, unused_step), unused_ys = lax.scan(
        forward_step, (grouped, zero_block, zero_block, jnp.int32(0)), None, length=section_count
    )
    first_saved = lax.cond(
        section_idx == section_count - 1, lambda: precompute(kept), lambda: zero_proj
    )

    def backward_step(carry, unused):
        upstream, grad_sum, step, saved = carry
        active = section_idx == step

        def differentiate():
            return layer_backward(
                kept, steering, saved, upstream, gain_row, full_qkv, full_out, tables, allowed
            )

        grad_in, steer_part = lax.cond(
            active, differentiate, lambda: (zero_block, jnp.zeros_like(steering))
        )
        sent = lax.ppermute(grad_in, "section", backward_route)
        next_saved = lax.cond(section_idx == step - 1, lambda: precompute(kept), lambda: zero_proj)
        return ((sent, grad_sum + steer_part, step - 1, next_saved), None)

    (unused_grad, grad_sum, unused_step, unused_saved), unused_zs = lax.scan(
        backward_step,
        (cotangent, jnp.zeros_like(steering), jnp.int32(section_count - 1), first_saved),
        None,
        length=section_count,
    )
    total = butterfly_sum(grad_sum, "dp")
    return (produced.reshape(1, micro_count, row_count, width), total[None])


def solution(mesh):
    in_specs = (
        P(None, "dp", None),
        P(),
        P(None, "dp"),
        P(None, "dp", None),
        P("section", None),
        P("section", None),
        P("section", "dp", None),
        P("section", "dp", None),
        P("section", None, "dp"),
    )
    out_specs = (P("section", None, "dp", None), P("section", None))
    return jax.shard_map(body, mesh=mesh, in_specs=in_specs, out_specs=out_specs, check_vma=False)
```

profile of v0, /device:TPU:2, one launch (start us, length us, event | category | flops | bytes accessed | tf_op | source)
XLA Modules:
  0.0 510.0 jit_solution(17521883404294243884)
XLA Ops:
  8.0 1.6 pad_maximum_fusion.5
  10.9 2.9 convert_reduce_fusion.4
  13.9 1.1 convolution_convert_fusion.8
  15.2 1.1 convolution_convert_fusion.7
  16.5 1.1 convolution_convert_fusion.6
  17.9 1.1 convolution_convert_fusion.5
  19.2 2.4 pad_maximum_fusion.3
  21.6 11.7 %all-to-all-start = ((bf16[32,4,2,2048]{3,2,1,0:T(2,128)(2,1)}), bf16[32,4,2,2048]{3,2,1,0:T(2,128)(2,1)S(1)}, u32[]{:S(2)}, u32[]{:S(2)}) async-start(bf16[32,4,2,2048]{3,2,1,0:T(2,128)(2,1)} %pad_maximum_fusion.3), calls=%async_computation | async-start | bytes 2097152 | tf_op jit(solution)/shard_map/all_to_all | solution.py:198
  38.0 27.3 %all-to-all-done = bf16[32,4,2,2048]{3,2,1,0:T(2,128)(2,1)S(1)} async-done(((bf16[32,4,2,2048]{3,2,1,0:T(2,128)(2,1)}), bf16[32,4,2,2048]{3,2,1,0:T(2,128)(2,1)S(1)}, u32[]{:S(2)}, u32[]{:S(2)}) %all-to-all-start) | async-done | bytes 1048608 | tf_op jit(solution)/shard_map/all_to_all | solution.py:198
  67.5 31.5 %all-gather.6.cloned.1.call-done = bf16[1,1024,2048]{1,2,0:T(8,128)(2,1)} async-done(((bf16[1,1024,64]{1,2,0:T(8,128)(2,1)}), bf16[1,1024,2048]{1,2,0:T(8,128)(2,1)}) %all-gather.6.cloned.1.call-update) | async-done | bytes 4194320 | tf_op jit(solution)/shard_map/all_gather | solution.py:182
  99.0 6.5 %copy.55 = bf16[1024,2048]{1,0:T(8,128)(2,1)} copy(bf16[1024,2048]{0,1:T(8,128)(2,1)} %bitcast.223) | data formatting | bytes 8388608
  105.6 81.7 %all-gather.4.cloned.1.call-done = bf16[2048,1536]{1,0:T(8,128)(2,1)} async-done(((bf16[64,1536]{1,0:T(8,128)(2,1)}), bf16[2048,1536]{1,0:T(8,128)(2,1)}) %all-gather.4.cloned.1.call-update) | async-done | bytes 6291472 | tf_op jit(solution)/shard_map/all_gather | solution.py:179
  187.3 115.0 %while.42 = (s32[]{:T(128)}, bf16[128,2048]{1,0:T(8,128)(2,1)S(1)}, bf16[128,2048]{1,0:T(8,128)(2,1)S(1)}, bf16[128,2048]{1,0:T(8,128)(2,1)S(1)}, s32[]{:T(128)}...) while((s32[]{:T(128)}, bf16[128,2048]{1,0:T(8,128)(2,1)S(1)}, ...), condition=%wide.region_14.15_spmd.clone.clone.clone, body=%wide.region_8.14_spmd.clone.clone.clone.sunk | while | flops 1451809152 | bytes 27381680 | solution.py:238
  188.1 1.9 collective-permute-start
  190.4 8.2 %collective-permute-done = bf16[128,2048]{1,0:T(8,128)(2,1)S(1)} collective-permute-done((bf16[128,2048]{1,0:T(8,128)(2,1)S(1)}, bf16[128,2048]{1,0:T(8,128)(2,1)S(1)}, u32[]{:S(2)}, u32[]{:S(2)}) %collective-permute-start) | collective-permute-done | bytes 524320 | tf_op jit(solution)/shard_map/while/body/eval_jaxpr/ppermute | solution.py:235
  199.6 1.9 collective-permute-start
  201.9 18.8 %collective-permute-done = bf16[128,2048]{1,0:T(8,128)(2,1)S(1)} collective-permute-done((bf16[128,2048]{1,0:T(8,128)(2,1)S(1)}, bf16[128,2048]{1,0:T(8,128)(2,1)S(1)}, u32[]{:S(2)}, u32[]{:S(2)}) %collective-permute-start) | collective-permute-done | bytes 524320 | tf_op jit(solution)/shard_map/while/body/eval_jaxpr/ppermute | solution.py:235
  221.5 9.8 %conditional.17 = (bf16[128,2048]{1,0:T(8,128)(2,1)S(1)}) conditional(s32[]{:T(128)} %convert_element_type.348, () %tuple.183, (bf16[128,2048]{1,0:T(8,128)(2,1)S(1)}, f32[1,2048]{1,0:T(1,128)S(1)}, f32[1,2048]{1,0:T(1,128)S(1)}, bf16[2048,1536]{1,0:T(8,128)(2,1)}, s32[128]{0:T(128)}, /*index=5*/f32[128,1,32]{0,2,1:T(8,128)S(1)}, ...), branch_computations={%region_9.9_spmd, %region_10.13_spmd} | conditional | flops 1450756480 | bytes 20941832 | solution.py:233
  221.7 3.8 fusion.18
  228.4 2.9 fusion.13
  231.3 1.9 collective-permute-start
  233.6 8.2 %collective-permute-done = bf16[128,2048]{1,0:T(8,128)(2,1)S(1)} collective-permute-done((bf16[128,2048]{1,0:T(8,128)(2,1)S(1)}, bf16[128,2048]{1,0:T(8,128)(2,1)S(1)}, u32[]{:S(2)}, u32[]{:S(2)}) %collective-permute-start) | collective-permute-done | bytes 524320 | tf_op jit(solution)/shard_map/while/body/eval_jaxpr/ppermute | solution.py:235
  242.7 5.0 collective-permute-start
  248.1 5.2 %collective-permute-done = bf16[128,2048]{1,0:T(8,128)(2,1)S(1)} collective-permute-done((bf16[128,2048]{1,0:T(8,128)(2,1)S(1)}, bf16[128,2048]{1,0:T(8,128)(2,1)S(1)}, u32[]{:S(2)}, u32[]{:S(2)}) %collective-permute-start) | collective-permute-done | bytes 524320 | tf_op jit(solution)/shard_map/while/body/eval_jaxpr/ppermute | solution.py:235
  254.2 2.5 collective-permute-start
  257.0 7.6 %collective-permute-done = bf16[128,2048]{1,0:T(8,128)(2,1)S(1)} collective-permute-done((bf16[128,2048]{1,0:T(8,128)(2,1)S(1)}, bf16[128,2048]{1,0:T(8,128)(2,1)S(1)}, u32[]{:S(2)}, u32[]{:S(2)}) %collective-permute-start) | collective-permute-done | bytes 524320 | tf_op jit(solution)/shard_map/while/body/eval_jaxpr/ppermute | solution.py:235
  265.6 12.2 %collective-permute-start = (bf16[128,2048]{1,0:T(8,128)(2,1)S(1)}, bf16[128,2048]{1,0:T(8,128)(2,1)S(1)}, u32[]{:S(2)}, u32[]{:S(2)}) collective-permute-start(bf16[128,2048]{1,0:T(8,128)(2,1)S(1)} %get-tuple-element.1353), channel_id=1, source_target_pairs={{0,32},{32,64},{64,96},{96,128},{128,160},{160,192},{192,224},{1,3... | collective-permute-start | bytes 1572872 | tf_op jit(solution)/shard_map/while/body/eval_jaxpr/ppermute | solution.py:235
  278.2 1.1 collective-permute-done
  280.3 9.0 %collective-permute-start = (bf16[128,2048]{1,0:T(8,128)(2,1)S(1)}, bf16[128,2048]{1,0:T(8,128)(2,1)S(1)}, u32[]{:S(2)}, u32[]{:S(2)}) collective-permute-start(bf16[128,2048]{1,0:T(8,128)(2,1)S(1)} %get-tuple-element.1353), channel_id=1, source_target_pairs={{0,32},{32,64},{64,96},{96,128},{128,160},{160,192},{192,224},{1,3... | collective-permute-start | bytes 1572872 | tf_op jit(solution)/shard_map/while/body/eval_jaxpr/ppermute | solution.py:235
  289.6 1.1 collective-permute-done
  291.7 9.0 %collective-permute-start = (bf16[128,2048]{1,0:T(8,128)(2,1)S(1)}, bf16[128,2048]{1,0:T(8,128)(2,1)S(1)}, u32[]{:S(2)}, u32[]{:S(2)}) collective-permute-start(bf16[128,2048]{1,0:T(8,128)(2,1)S(1)} %get-tuple-element.1353), channel_id=1, source_target_pairs={{0,32},{32,64},{64,96},{96,128},{128,160},{160,192},{192,224},{1,3... | collective-permute-start | bytes 1572872 | tf_op jit(solution)/shard_map/while/body/eval_jaxpr/ppermute | solution.py:235
  301.0 1.1 collective-permute-done
  303.7 174.6 %while.43 = (s32[]{:T(128)}, bf16[128,2048]{1,0:T(8,128)(2,1)S(1)}, f32[2048]{0:T(1024)S(1)}, f32[128,1536]{1,0:T(8,128)}, s32[]{:T(128)}, /*index=5*/bf16[1024,...) while((s32[]{:T(128)}, bf16[128,2048]{1,0:T(8,128)(2,1)S(1)}, ...), condition=%wide.region_32.33_spmd.clone.clone.clone, body=%wide.region_18.32_spmd.clone.clone.clone.sunk | while | flops 2336233984 | bytes 65241192 | solution.py:261
  304.6 1.9 collective-permute-start.1
  307.5 7.5 %collective-permute-done.1 = bf16[128,2048]{1,0:T(8,128)(2,1)S(1)} collective-permute-done((bf16[128,2048]{1,0:T(8,128)(2,1)S(1)}, bf16[128,2048]{1,0:T(8,128)(2,1)S(1)}, u32[]{:S(2)}, u32[]{:S(2)}) %collective-permute-start.1) | collective-permute-done | bytes 524320 | tf_op jit(solution)/shard_map/while/body/eval_jaxpr/ppermute | solution.py:257
  315.8 2.0 collective-permute-start.1
  318.9 11.4 %collective-permute-done.1 = bf16[128,2048]{1,0:T(8,128)(2,1)S(1)} collective-permute-done((bf16[128,2048]{1,0:T(8,128)(2,1)S(1)}, bf16[128,2048]{1,0:T(8,128)(2,1)S(1)}, u32[]{:S(2)}, u32[]{:S(2)}) %collective-permute-start.1) | collective-permute-done | bytes 524320 | tf_op jit(solution)/shard_map/while/body/eval_jaxpr/ppermute | solution.py:257
  331.2 1.9 collective-permute-start.1
  334.1 7.6 %collective-permute-done.1 = bf16[128,2048]{1,0:T(8,128)(2,1)S(1)} collective-permute-done((bf16[128,2048]{1,0:T(8,128)(2,1)S(1)}, bf16[128,2048]{1,0:T(8,128)(2,1)S(1)}, u32[]{:S(2)}, u32[]{:S(2)}) %collective-permute-start.1) | collective-permute-done | bytes 524320 | tf_op jit(solution)/shard_map/while/body/eval_jaxpr/ppermute | solution.py:257
  342.5 1.9 collective-permute-start.1
  345.4 8.2 %collective-permute-done.1 = bf16[128,2048]{1,0:T(8,128)(2,1)S(1)} collective-permute-done((bf16[128,2048]{1,0:T(8,128)(2,1)S(1)}, bf16[128,2048]{1,0:T(8,128)(2,1)S(1)}, u32[]{:S(2)}, u32[]{:S(2)}) %collective-permute-start.1) | collective-permute-done | bytes 524320 | tf_op jit(solution)/shard_map/while/body/eval_jaxpr/ppermute | solution.py:257
  354.5 1.9 collective-permute-start.1
  356.5 5.0 conditional.19
  356.7 4.7 fusion.69
  361.4 59.3 %collective-permute-done.1 = bf16[128,2048]{1,0:T(8,128)(2,1)S(1)} collective-permute-done((bf16[128,2048]{1,0:T(8,128)(2,1)S(1)}, bf16[128,2048]{1,0:T(8,128)(2,1)S(1)}, u32[]{:S(2)}, u32[]{:S(2)}) %collective-permute-start.1) | collective-permute-done | bytes 524320 | tf_op jit(solution)/shard_map/while/body/eval_jaxpr/ppermute | solution.py:257
  421.5 12.8 %conditional.18 = (bf16[128,2048]{1,0:T(8,128)(2,1)S(1)}, f32[2048]{0:T(1024)S(1)}) conditional(s32[]{:T(128)} %convert_element_type.349, () %tuple.186, (bf16[128,2048]{1,0:T(8,128)(2,1)S(1)}, bf16[1024,2048]{1,0:T(8,128)(2,1)}, s32[128]{0:T(128)}, f32[128,1536]{1,0:T(8,128)}, f32[128,1,32]{0,2,1:T(8,128)S(1)}, ...), branch_computations={%region_19.19_spmd, %region_20.28_spmd} | conditional | flops 1528560128 | bytes 54817856 | solution.py:254
  422.4 3.7 convolution_convert_fusion.4
  426.3 1.4 copy.50
  431.6 2.3 multiply_reduce_fusion.3
  434.3 1.9 collective-permute-start.1
  437.2 5.7 %collective-permute-done.1 = bf16[128,2048]{1,0:T(8,128)(2,1)S(1)} collective-permute-done((bf16[128,2048]{1,0:T(8,128)(2,1)S(1)}, bf16[128,2048]{1,0:T(8,128)(2,1)S(1)}, u32[]{:S(2)}, u32[]{:S(2)}) %collective-permute-start.1) | collective-permute-done | bytes 524320 | tf_op jit(solution)/shard_map/while/body/eval_jaxpr/ppermute | solution.py:257
  443.7 16.5 %collective-permute-start.1 = (bf16[128,2048]{1,0:T(8,128)(2,1)S(1)}, bf16[128,2048]{1,0:T(8,128)(2,1)S(1)}, u32[]{:S(2)}, u32[]{:S(2)}) collective-permute-start(bf16[128,2048]{1,0:T(8,128)(2,1)S(1)} %get-tuple-element.1250), channel_id=1, source_target_pairs={{32,0},{64,32},{96,64},{128,96},{160,128},{192,160},{224,192},{33,... | collective-permute-start | bytes 1572872 | tf_op jit(solution)/shard_map/while/body/eval_jaxpr/ppermute | solution.py:257
  461.2 5.7 %collective-permute-done.1 = bf16[128,2048]{1,0:T(8,128)(2,1)S(1)} collective-permute-done((bf16[128,2048]{1,0:T(8,128)(2,1)S(1)}, bf16[128,2048]{1,0:T(8,128)(2,1)S(1)}, u32[]{:S(2)}, u32[]{:S(2)}) %collective-permute-start.1) | collective-permute-done | bytes 524320 | tf_op jit(solution)/shard_map/while/body/eval_jaxpr/ppermute | solution.py:257
  467.8 3.8 collective-permute-start.1
  472.6 5.7 %collective-permute-done.1 = bf16[128,2048]{1,0:T(8,128)(2,1)S(1)} collective-permute-done((bf16[128,2048]{1,0:T(8,128)(2,1)S(1)}, bf16[128,2048]{1,0:T(8,128)(2,1)S(1)}, u32[]{:S(2)}, u32[]{:S(2)}) %collective-permute-start.1) | collective-permute-done | bytes 524320 | tf_op jit(solution)/shard_map/while/body/eval_jaxpr/ppermute | solution.py:257
  478.3 2.7 collective-permute-start.4
  481.2 1.4 collective-permute-start.2
  483.7 1.8 collective-permute-done.3
  485.6 2.2 collective-permute-start.7
  487.8 1.8 collective-permute-start.6
  489.6 3.5 collective-permute-start.5
  494.2 3.0 collective-permute-done.5
  497.2 1.5 collective-permute-start.8
  498.8 3.7 collective-permute-done.8
  (242 shorter events, 54.6 us)
Async XLA Ops:
  7.2 26.1 %copy-start.5 = (s32[4,32]{1,0:T(4,128)S(1)}, s32[4,32]{1,0:T(4,128)}, u32[]{:S(2)}) copy-start(s32[4,32]{1,0:T(4,128)} %param.23) | copy-start | bytes 1540
  7.2 91.9 %all-gather.6.cloned.1.call-start = ((), (), s32[]{:S(2)}) async-start(), calls=%async_computation.2 | async-start | bytes 4325376 | tf_op jit(solution)/shard_map/all_gather | solution.py:182
  7.9 179.4 %all-gather.4.cloned.1.call-start = ((), (), s32[]{:S(2)}) async-start(), calls=%async_computation.1 | async-start | bytes 6488064 | tf_op jit(solution)/shard_map/all_gather | solution.py:179
  21.6 43.7 %all-to-all-start = ((bf16[32,4,2,2048]{3,2,1,0:T(2,128)(2,1)}), bf16[32,4,2,2048]{3,2,1,0:T(2,128)(2,1)S(1)}, u32[]{:S(2)}, u32[]{:S(2)}) async-start(bf16[32,4,2,2048]{3,2,1,0:T(2,128)(2,1)} %pad_maximum_fusion.3), calls=%async_computation | async-start | bytes 2097152 | tf_op jit(solution)/shard_map/all_to_all | solution.py:198
  66.2 121.1 %copy-start.2 = (f32[1,2048]{1,0:T(1,128)S(1)}, f32[1,2048]{1,0:T(1,128)}, u32[]{:S(2)}) copy-start(f32[1,2048]{1,0:T(1,128)} %param.26) | copy-start | bytes 24580
  66.2 121.1 %copy-start.3 = (f32[1,2048]{1,0:T(1,128)S(1)}, f32[1,2048]{1,0:T(1,128)}, u32[]{:S(2)}) copy-start(f32[1,2048]{1,0:T(1,128)} %param.25) | copy-start | bytes 24580
  188.1 10.5 %collective-permute-start = (bf16[128,2048]{1,0:T(8,128)(2,1)S(1)}, bf16[128,2048]{1,0:T(8,128)(2,1)S(1)}, u32[]{:S(2)}, u32[]{:S(2)}) collective-permute-start(bf16[128,2048]{1,0:T(8,128)(2,1)S(1)} %get-tuple-element.1353), channel_id=1, source_target_pairs={{0,32},{32,64},{64,96},{96,128},{128,160},{160,192},{192,224},{1,3... | collective-permute-start | bytes 1572872 | tf_op jit(solution)/shard_map/while/body/eval_jaxpr/ppermute | solution.py:235
  199.6 21.1 %collective-permute-start = (bf16[128,2048]{1,0:T(8,128)(2,1)S(1)}, bf16[128,2048]{1,0:T(8,128)(2,1)S(1)}, u32[]{:S(2)}, u32[]{:S(2)}) collective-permute-start(bf16[128,2048]{1,0:T(8,128)(2,1)S(1)} %get-tuple-element.1353), channel_id=1, source_target_pairs={{0,32},{32,64},{64,96},{96,128},{128,160},{160,192},{192,224},{1,3... | collective-permute-start | bytes 1572872 | tf_op jit(solution)/shard_map/while/body/eval_jaxpr/ppermute | solution.py:235
  231.3 10.5 %collective-permute-start = (bf16[128,2048]{1,0:T(8,128)(2,1)S(1)}, bf16[128,2048]{1,0:T(8,128)(2,1)S(1)}, u32[]{:S(2)}, u32[]{:S(2)}) collective-permute-start(bf16[128,2048]{1,0:T(8,128)(2,1)S(1)} %get-tuple-element.1353), channel_id=1, source_target_pairs={{0,32},{32,64},{64,96},{96,128},{128,160},{160,192},{192,224},{1,3... | collective-permute-start | bytes 1572872 | tf_op jit(solution)/shard_map/while/body/eval_jaxpr/ppermute | solution.py:235
  242.7 10.5 %collective-permute-start = (bf16[128,2048]{1,0:T(8,128)(2,1)S(1)}, bf16[128,2048]{1,0:T(8,128)(2,1)S(1)}, u32[]{:S(2)}, u32[]{:S(2)}) collective-permute-start(bf16[128,2048]{1,0:T(8,128)(2,1)S(1)} %get-tuple-element.1353), channel_id=1, source_target_pairs={{0,32},{32,64},{64,96},{96,128},{128,160},{160,192},{192,224},{1,3... | collective-permute-start | bytes 1572872 | tf_op jit(solution)/shard_map/while/body/eval_jaxpr/ppermute | solution.py:235
  254.2 10.5 %collective-permute-start = (bf16[128,2048]{1,0:T(8,128)(2,1)S(1)}, bf16[128,2048]{1,0:T(8,128)(2,1)S(1)}, u32[]{:S(2)}, u32[]{:S(2)}) collective-permute-start(bf16[128,2048]{1,0:T(8,128)(2,1)S(1)} %get-tuple-element.1353), channel_id=1, source_target_pairs={{0,32},{32,64},{64,96},{96,128},{128,160},{160,192},{192,224},{1,3... | collective-permute-start | bytes 1572872 | tf_op jit(solution)/shard_map/while/body/eval_jaxpr/ppermute | solution.py:235
  265.6 13.7 %collective-permute-start = (bf16[128,2048]{1,0:T(8,128)(2,1)S(1)}, bf16[128,2048]{1,0:T(8,128)(2,1)S(1)}, u32[]{:S(2)}, u32[]{:S(2)}) collective-permute-start(bf16[128,2048]{1,0:T(8,128)(2,1)S(1)} %get-tuple-element.1353), channel_id=1, source_target_pairs={{0,32},{32,64},{64,96},{96,128},{128,160},{160,192},{192,224},{1,3... | collective-permute-start | bytes 1572872 | tf_op jit(solution)/shard_map/while/body/eval_jaxpr/ppermute | solution.py:235
  280.3 10.5 %collective-permute-start = (bf16[128,2048]{1,0:T(8,128)(2,1)S(1)}, bf16[128,2048]{1,0:T(8,128)(2,1)S(1)}, u32[]{:S(2)}, u32[]{:S(2)}) collective-permute-start(bf16[128,2048]{1,0:T(8,128)(2,1)S(1)} %get-tuple-element.1353), channel_id=1, source_target_pairs={{0,32},{32,64},{64,96},{96,128},{128,160},{160,192},{192,224},{1,3... | collective-permute-start | bytes 1572872 | tf_op jit(solution)/shard_map/while/body/eval_jaxpr/ppermute | solution.py:235
  291.7 10.5 %collective-permute-start = (bf16[128,2048]{1,0:T(8,128)(2,1)S(1)}, bf16[128,2048]{1,0:T(8,128)(2,1)S(1)}, u32[]{:S(2)}, u32[]{:S(2)}) collective-permute-start(bf16[128,2048]{1,0:T(8,128)(2,1)S(1)} %get-tuple-element.1353), channel_id=1, source_target_pairs={{0,32},{32,64},{64,96},{96,128},{128,160},{160,192},{192,224},{1,3... | collective-permute-start | bytes 1572872 | tf_op jit(solution)/shard_map/while/body/eval_jaxpr/ppermute | solution.py:235
  302.2 1.4 copy-start.1
  302.3 1.4 copy-start
  302.3 1.4 copy-start.4
  304.6 10.4 %collective-permute-start.1 = (bf16[128,2048]{1,0:T(8,128)(2,1)S(1)}, bf16[128,2048]{1,0:T(8,128)(2,1)S(1)}, u32[]{:S(2)}, u32[]{:S(2)}) collective-permute-start(bf16[128,2048]{1,0:T(8,128)(2,1)S(1)} %get-tuple-element.1250), channel_id=1, source_target_pairs={{32,0},{64,32},{96,64},{128,96},{160,128},{192,160},{224,192},{33,... | collective-permute-start | bytes 1572872 | tf_op jit(solution)/shard_map/while/body/eval_jaxpr/ppermute | solution.py:257
  315.8 14.5 %collective-permute-start.1 = (bf16[128,2048]{1,0:T(8,128)(2,1)S(1)}, bf16[128,2048]{1,0:T(8,128)(2,1)S(1)}, u32[]{:S(2)}, u32[]{:S(2)}) collective-permute-start(bf16[128,2048]{1,0:T(8,128)(2,1)S(1)} %get-tuple-element.1250), channel_id=1, source_target_pairs={{32,0},{64,32},{96,64},{128,96},{160,128},{192,160},{224,192},{33,... | collective-permute-start | bytes 1572872 | tf_op jit(solution)/shard_map/while/body/eval_jaxpr/ppermute | solution.py:257
  331.2 10.5 %collective-permute-start.1 = (bf16[128,2048]{1,0:T(8,128)(2,1)S(1)}, bf16[128,2048]{1,0:T(8,128)(2,1)S(1)}, u32[]{:S(2)}, u32[]{:S(2)}) collective-permute-start(bf16[128,2048]{1,0:T(8,128)(2,1)S(1)} %get-tuple-element.1250), channel_id=1, source_target_pairs={{32,0},{64,32},{96,64},{128,96},{160,128},{192,160},{224,192},{33,... | collective-permute-start | bytes 1572872 | tf_op jit(solution)/shard_map/while/body/eval_jaxpr/ppermute | solution.py:257
  342.5 11.1 %collective-permute-start.1 = (bf16[128,2048]{1,0:T(8,128)(2,1)S(1)}, bf16[128,2048]{1,0:T(8,128)(2,1)S(1)}, u32[]{:S(2)}, u32[]{:S(2)}) collective-permute-start(bf16[128,2048]{1,0:T(8,128)(2,1)S(1)} %get-tuple-element.1250), channel_id=1, source_target_pairs={{32,0},{64,32},{96,64},{128,96},{160,128},{192,160},{224,192},{33,... | collective-permute-start | bytes 1572872 | tf_op jit(solution)/shard_map/while/body/eval_jaxpr/ppermute | solution.py:257
  354.5 66.2 %collective-permute-start.1 = (bf16[128,2048]{1,0:T(8,128)(2,1)S(1)}, bf16[128,2048]{1,0:T(8,128)(2,1)S(1)}, u32[]{:S(2)}, u32[]{:S(2)}) collective-permute-start(bf16[128,2048]{1,0:T(8,128)(2,1)S(1)} %get-tuple-element.1250), channel_id=1, source_target_pairs={{32,0},{64,32},{96,64},{128,96},{160,128},{192,160},{224,192},{33,... | collective-permute-start | bytes 1572872 | tf_op jit(solution)/shard_map/while/body/eval_jaxpr/ppermute | solution.py:257
  428.5 2.7 slice-start
  429.3 2.2 slice-start.1
  434.3 8.6 %collective-permute-start.1 = (bf16[128,2048]{1,0:T(8,128)(2,1)S(1)}, bf16[128,2048]{1,0:T(8,128)(2,1)S(1)}, u32[]{:S(2)}, u32[]{:S(2)}) collective-permute-start(bf16[128,2048]{1,0:T(8,128)(2,1)S(1)} %get-tuple-element.1250), channel_id=1, source_target_pairs={{32,0},{64,32},{96,64},{128,96},{160,128},{192,160},{224,192},{33,... | collective-permute-start | bytes 1572872 | tf_op jit(solution)/shard_map/while/body/eval_jaxpr/ppermute | solution.py:257
  443.7 23.2 %collective-permute-start.1 = (bf16[128,2048]{1,0:T(8,128)(2,1)S(1)}, bf16[128,2048]{1,0:T(8,128)(2,1)S(1)}, u32[]{:S(2)}, u32[]{:S(2)}) collective-permute-start(bf16[128,2048]{1,0:T(8,128)(2,1)S(1)} %get-tuple-element.1250), channel_id=1, source_target_pairs={{32,0},{64,32},{96,64},{128,96},{160,128},{192,160},{224,192},{33,... | collective-permute-start | bytes 1572872 | tf_op jit(solution)/shard_map/while/body/eval_jaxpr/ppermute | solution.py:257
  467.8 10.5 %collective-permute-start.1 = (bf16[128,2048]{1,0:T(8,128)(2,1)S(1)}, bf16[128,2048]{1,0:T(8,128)(2,1)S(1)}, u32[]{:S(2)}, u32[]{:S(2)}) collective-permute-start(bf16[128,2048]{1,0:T(8,128)(2,1)S(1)} %get-tuple-element.1250), channel_id=1, source_target_pairs={{32,0},{64,32},{96,64},{128,96},{160,128},{192,160},{224,192},{33,... | collective-permute-start | bytes 1572872 | tf_op jit(solution)/shard_map/while/body/eval_jaxpr/ppermute | solution.py:257
  478.3 5.4 %collective-permute-start.4 = (f32[2048]{0:T(1024)S(1)}, f32[2048]{0:T(1024)S(1)}, u32[]{:S(2)}, u32[]{:S(2)}) collective-permute-start(f32[2048]{0:T(1024)S(1)} %get-tuple-element.619), channel_id=1, source_target_pairs={{0,3},{1,2},{2,1},{3,0},{4,7},{5,6},{6,5},{7,4},{8,11},{9,10},{10,... | collective-permute-start | bytes 24584 | tf_op jit(solution)/shard_map/ppermute | solution.py:128
  481.0 4.5 collective-permute-start.3
  481.2 4.3 collective-permute-start.2
  485.6 8.5 %collective-permute-start.7 = (f32[2048]{0:T(1024)S(1)}, f32[2048]{0:T(1024)S(1)}, u32[]{:S(2)}, u32[]{:S(2)}) collective-permute-start(f32[2048]{0:T(1024)S(1)} %bitcast.245), channel_id=1, source_target_pairs={{0,12},{1,13},{2,14},{3,15},{4,8},{5,9},{6,10},{7,11},{8,4},{9,5},... | collective-permute-start | bytes 24584 | tf_op jit(solution)/shard_map/ppermute | solution.py:128
  487.8 6.4 %collective-permute-start.6 = (f32[2048]{0:T(1024)S(1)}, f32[2048]{0:T(1024)S(1)}, u32[]{:S(2)}, u32[]{:S(2)}) collective-permute-start(f32[2048]{0:T(1024)S(1)} %bitcast.246), channel_id=1, source_target_pairs={{0,8},{1,9},{2,10},{3,11},{4,12},{5,13},{6,14},{7,15},{8,0},{9,1},... | collective-permute-start | bytes 24584 | tf_op jit(solution)/shard_map/ppermute | solution.py:128
  489.6 7.6 %collective-permute-start.5 = (f32[2048]{0:T(1024)S(1)}, f32[2048]{0:T(1024)S(1)}, u32[]{:S(2)}, u32[]{:S(2)}) collective-permute-start(f32[2048]{0:T(1024)S(1)} %bitcast.247), channel_id=1, source_target_pairs={{0,4},{1,5},{2,6},{3,7},{4,0},{5,1},{6,2},{7,3},{8,12},{9,13},{10,... | collective-permute-start | bytes 24584 | tf_op jit(solution)/shard_map/ppermute | solution.py:128
  497.2 5.2 %collective-permute-start.8 = (f32[2048]{0:T(1024)S(1)}, f32[2048]{0:T(1024)S(1)}, u32[]{:S(2)}, u32[]{:S(2)}) collective-permute-start(f32[2048]{0:T(1024)S(1)} %bitcast.244), channel_id=1, source_target_pairs={{0,16},{1,17},{2,18},{3,19},{4,20},{5,21},{6,22},{7,23},{8,24},{9,... | collective-permute-start | bytes 24584 | tf_op jit(solution)/shard_map/ppermute | solution.py:128
Sparse Core Ops, SparseCore 0:
  10.6 88.4 all-gather.5
  102.2 85.0 all-gather.3
where the time goes:
time: 511 us; the launch traced here: 510 us
  waiting for transfers between devices  314 us (61%)
  starting transfers between devices  100 us (20%)
  other arithmetic  31.1 us (6%)
  matrix products  25.8 us (5%)
  local copies, waits for them, and re-layouts  22.5 us (4%)
  between operations  14.4 us (3%)
    ppermute x8, waiting for transfers between devices, backward_step(): sent = lax.ppermute(grad_in, 'section', backward_route)  111 us
    all_gather x1, waiting for transfers between devices, body(): lax.all_gather(jnp.concatenate([w_query[0], w_keyval[0]], axis=1), 'dp',...  81.7 us
    ppermute x8, waiting for transfers between devices, forward_step(): sent = lax.ppermute(hidden_new, 'section', forward_route)  51.4 us
    ppermute x8, starting transfers between devices, forward_step(): sent = lax.ppermute(hidden_new, 'section', forward_route)  43.4 us
    ppermute x8, starting transfers between devices, backward_step(): sent = lax.ppermute(grad_in, 'section', backward_route)  32 us
    all_gather x1, waiting for transfers between devices, body(): full_out = lax.all_gather(w_out[0], 'dp', axis=1, tiled=True)  31.5 us
    all_to_all x1, waiting for transfers between devices, body(): lax.all_to_all(packed, 'dp', split_axis=0, concat_axis=0, tiled=True)  27.3 us
    ppermute x7, starting transfers between devices, butterfly_sum(): received.append(lax.ppermute(values, axis, route))  13.4 us
  transfers between devices with their start and end apart: 26, of which 24 were waited for; matrix products, arithmetic and copies ran while one was open for 8% of the time, Pallas kernels for 0%

commit v1 on v0

--- a/solution.py
+++ b/solution.py
@@ -179,7 +179,13 @@
     full_qkv = lax.all_gather(
         jnp.concatenate([w_query[0], w_keyval[0]], axis=1), "dp", axis=0, tiled=True
     )
-    full_out = lax.all_gather(w_out[0], "dp", axis=1, tiled=True)
+    x_in = w_out[0]
+    full_out = jnp.concatenate(
+        jax.lax.all_to_all(
+            jnp.stack([x_in] * jax.lax.axis_size("dp")), axis_name="dp", split_axis=0, concat_axis=0
+        ),
+        axis=1,
+    )
     gain_row = gain[0]
     steering = steer[0]
     plans = [

time: 511 us -> 553 us (1.082)
  blocking collectives: 0 us -> 45.9 us
  waiting for transfers between devices: 314 us -> 282 us
  other arithmetic: 31.1 us -> 48.6 us
  local copies, waits for them, and re-layouts: 22.5 us -> 30.8 us
    all_to_all x1, waiting for transfers between devices: 27.3 us -> 115 us  [body(): jax.lax.all_to_all(jnp.stack([x_in] * jax.lax.axis_size('dp')), axis_name...]
    all_gather x1, waiting for transfers between devices: 81.7 us -> 0.01 us  [body(): lax.all_gather(jnp.concatenate([w_query[0], w_keyval[0]], axis=1), 'dp',...]
    all_to_all x0 -> x1, blocking collectives: none -> 45.9 us  [body(): lax.all_to_all(packed, 'dp', split_axis=0, concat_axis=0, tiled=True)]
    all_gather x1 -> x0, waiting for transfers between devices: 31.5 us -> none  [body(): full_out = lax.all_gather(w_out[0], 'dp', axis=1, tiled=True)]
    select_n x8, other arithmetic: 2.87 us -> 16.3 us  [forward_step(): produced = jnp.where(active, hidden_new, produced)]
    ppermute x8, waiting for transfers between devices: 51.4 us -> 39.9 us  [forward_step(): sent = lax.ppermute(hidden_new, 'section', forward_route)]
    ppermute x8, waiting for transfers between devices: 111 us -> 118 us  [backward_step(): sent = lax.ppermute(grad_in, 'section', backward_route)]
    all_to_all x1, starting transfers between devices: 11.7 us -> 5.04 us  [body(): jax.lax.all_to_all(jnp.stack([x_in] * jax.lax.axis_size('dp')), axis_name...]
  transfers between devices with their start and end apart: 26 -> 25, of which waited for: 24 -> 19; matrix products, arithmetic and copies ran while one was open for 8% -> 10% of each run, Pallas kernels for 0% -> 0%
where the time goes in v1:
time: 553 us; the launch traced here: 548 us
  waiting for transfers between devices  282 us (51%)
  starting transfers between devices  97.4 us (18%)
  other arithmetic  48.6 us (9%)
  blocking collectives  45.9 us (8%)
  local copies, waits for them, and re-layouts  30.8 us (6%)
  matrix products  27.8 us (5%)
  between operations  14.4 us (3%)
    ppermute x8, waiting for transfers between devices, backward_step(): sent = lax.ppermute(grad_in, 'section', backward_route)  118 us
    all_to_all x1, waiting for transfers between devices, body(): jax.lax.all_to_all(jnp.stack([x_in] * jax.lax.axis_size('dp')), axis_name...  115 us
    all_to_all x1, blocking collectives, body(): lax.all_to_all(packed, 'dp', split_axis=0, concat_axis=0, tiled=True)  45.9 us
    ppermute x8, waiting for transfers between devices, forward_step(): sent = lax.ppermute(hidden_new, 'section', forward_route)  39.9 us
    ppermute x8, starting transfers between devices, forward_step(): sent = lax.ppermute(hidden_new, 'section', forward_route)  39.5 us
    ppermute x8, starting transfers between devices, backward_step(): sent = lax.ppermute(grad_in, 'section', backward_route)  35.1 us
    ppermute x7, starting transfers between devices, butterfly_sum(): received.append(lax.ppermute(values, axis, route))  17.7 us
    mul x16, other arithmetic, rope_tables(): angles = positions.astype(jnp.float32)[..., None] * inverse  16.8 us
  transfers between devices with their start and end apart: 25, of which 19 were waited for; matrix products, arithmetic and copies ran while one was open for 10% of the time, Pallas kernels for 0%

profile of v1, /device:TPU:2, one launch (start us, length us, event | category | flops | bytes accessed | tf_op | source)
XLA Modules:
  0.0 548.4 jit_solution(8661053694967328984)
XLA Ops:
  7.2 1.7 pad_maximum_fusion.5
  10.2 2.9 convert_reduce_fusion.4
  18.5 1.6 pad_maximum_fusion.3
  20.1 45.9 %all_to_all.10 = bf16[32,4,2,2048]{3,2,1,0:T(2,128)(2,1)S(1)} all-to-all(bf16[32,4,2,2048]{3,2,1,0:T(2,128)(2,1)S(1)} %pad_maximum_fusion.3), channel_id=1, replica_groups=mesh['section'=8,'dp'=32] {'dp'}, dimensions={0} | all-to-all | bytes 2097152 | tf_op jit(solution)/shard_map/all_to_all | solution.py:204
  66.0 2.6 stack.62
  68.6 5.0 all-to-all-start.1
  80.8 115.5 %all-to-all-done.1 = bf16[32,1024,64]{1,2,0:T(8,128)(2,1)} async-done(((bf16[32,1024,64]{1,2,0:T(8,128)(2,1)}), bf16[32,1024,64]{1,2,0:T(8,128)(2,1)}, u32[]{:S(2)}, u32[]{:S(2)}) %all-to-all-start.1) | async-done | bytes 4194336 | tf_op jit(solution)/shard_map/all_to_all | solution.py:184
  196.2 6.5 %copy.56 = bf16[1024,2048]{1,0:T(8,128)(2,1)} copy(bf16[1024,2048]{0,1:T(8,128)(2,1)} %bitcast.77) | data formatting | bytes 8388608
  202.8 117.0 %while.42 = (s32[]{:T(128)}, bf16[128,2048]{1,0:T(8,128)(2,1)S(1)}, bf16[128,2048]{1,0:T(8,128)(2,1)S(1)}, bf16[128,2048]{1,0:T(8,128)(2,1)}, s32[]{:T(128)}, /*...) while((s32[]{:T(128)}, bf16[128,2048]{1,0:T(8,128)(2,1)S(1)}, ...), condition=%wide.region_14.15_spmd.clone.clone.clone, body=%wide.region_8.14_spmd.clone.clone.clone.sunk | while | flops 1451809152 | bytes 27449312 | solution.py:244
  204.3 1.9 collective-permute-start
  207.3 7.4 %collective-permute-done = bf16[128,2048]{1,0:T(8,128)(2,1)S(1)} collective-permute-done((bf16[128,2048]{1,0:T(8,128)(2,1)S(1)}, bf16[128,2048]{1,0:T(8,128)(2,1)S(1)}, u32[]{:S(2)}, u32[]{:S(2)}) %collective-permute-start) | collective-permute-done | bytes 524320 | tf_op jit(solution)/shard_map/while/body/eval_jaxpr/ppermute | solution.py:241
  216.3 1.9 collective-permute-start
  218.2 2.2 select_select_fusion.3
  220.4 15.7 %collective-permute-done = bf16[128,2048]{1,0:T(8,128)(2,1)S(1)} collective-permute-done((bf16[128,2048]{1,0:T(8,128)(2,1)S(1)}, bf16[128,2048]{1,0:T(8,128)(2,1)S(1)}, u32[]{:S(2)}, u32[]{:S(2)}) %collective-permute-start) | collective-permute-done | bytes 524320 | tf_op jit(solution)/shard_map/while/body/eval_jaxpr/ppermute | solution.py:241
  237.5 9.1 %conditional.17 = (bf16[128,2048]{1,0:T(8,128)(2,1)S(1)}) conditional(s32[]{:T(128)} %convert_element_type.348, () %tuple.185, (bf16[128,2048]{1,0:T(8,128)(2,1)S(1)}, f32[1,2048]{1,0:T(1,128)S(1)}, f32[1,2048]{1,0:T(1,128)S(1)}, bf16[2048,1536]{1,0:T(8,128)(2,1)}, s32[128]{0:T(128)}, /*index=5*/f32[128,1,32]{0,2,1:T(8,128)}, ...), branch_computations={%region_9.9_spmd, %region_10.13_spmd} | conditional | flops 1450756480 | bytes 21009472 | solution.py:239
  237.7 3.8 fusion.18
  243.7 2.9 fusion.13
  246.6 1.9 collective-permute-start
  248.6 2.2 select_select_fusion.3
  250.7 6.4 %collective-permute-done = bf16[128,2048]{1,0:T(8,128)(2,1)S(1)} collective-permute-done((bf16[128,2048]{1,0:T(8,128)(2,1)S(1)}, bf16[128,2048]{1,0:T(8,128)(2,1)S(1)}, u32[]{:S(2)}, u32[]{:S(2)}) %collective-permute-start) | collective-permute-done | bytes 524320 | tf_op jit(solution)/shard_map/while/body/eval_jaxpr/ppermute | solution.py:241
  258.6 4.3 collective-permute-start
  263.0 2.2 select_select_fusion.3
  265.1 4.0 collective-permute-done
  270.6 1.9 collective-permute-start
  272.6 2.2 select_select_fusion.3
  274.7 6.4 %collective-permute-done = bf16[128,2048]{1,0:T(8,128)(2,1)S(1)} collective-permute-done((bf16[128,2048]{1,0:T(8,128)(2,1)S(1)}, bf16[128,2048]{1,0:T(8,128)(2,1)S(1)}, u32[]{:S(2)}, u32[]{:S(2)}) %collective-permute-start) | collective-permute-done | bytes 524320 | tf_op jit(solution)/shard_map/while/body/eval_jaxpr/ppermute | solution.py:241
  282.7 10.9 %collective-permute-start = (bf16[128,2048]{1,0:T(8,128)(2,1)S(1)}, bf16[128,2048]{1,0:T(8,128)(2,1)S(1)}, u32[]{:S(2)}, u32[]{:S(2)}) collective-permute-start(bf16[128,2048]{1,0:T(8,128)(2,1)S(1)} %get-tuple-element.1378), channel_id=1, source_target_pairs={{0,32},{32,64},{64,96},{96,128},{128,160},{160,192},{192,224},{1,3... | collective-permute-start | bytes 1572872 | tf_op jit(solution)/shard_map/while/body/eval_jaxpr/ppermute | solution.py:241
  293.6 2.2 select_select_fusion.3
  297.3 8.3 %collective-permute-start = (bf16[128,2048]{1,0:T(8,128)(2,1)S(1)}, bf16[128,2048]{1,0:T(8,128)(2,1)S(1)}, u32[]{:S(2)}, u32[]{:S(2)}) collective-permute-start(bf16[128,2048]{1,0:T(8,128)(2,1)S(1)} %get-tuple-element.1378), channel_id=1, source_target_pairs={{0,32},{32,64},{64,96},{96,128},{128,160},{160,192},{192,224},{1,3... | collective-permute-start | bytes 1572872 | tf_op jit(solution)/shard_map/while/body/eval_jaxpr/ppermute | solution.py:241
  305.6 2.2 select_select_fusion.3
  309.3 8.3 %collective-permute-start = (bf16[128,2048]{1,0:T(8,128)(2,1)S(1)}, bf16[128,2048]{1,0:T(8,128)(2,1)S(1)}, u32[]{:S(2)}, u32[]{:S(2)}) collective-permute-start(bf16[128,2048]{1,0:T(8,128)(2,1)S(1)} %get-tuple-element.1378), channel_id=1, source_target_pairs={{0,32},{32,64},{64,96},{96,128},{128,160},{160,192},{192,224},{1,3... | collective-permute-start | bytes 1572872 | tf_op jit(solution)/shard_map/while/body/eval_jaxpr/ppermute | solution.py:241
  317.6 2.2 select_select_fusion.3
  320.9 193.1 %while.43 = (s32[]{:T(128)}, bf16[128,2048]{1,0:T(8,128)(2,1)S(1)}, f32[2048]{0:T(1024)}, f32[128,1536]{1,0:T(8,128)}, s32[]{:T(128)}, /*index=5*/bf16[1024,2048...) while((s32[]{:T(128)}, bf16[128,2048]{1,0:T(8,128)(2,1)S(1)}, ...), condition=%wide.region_32.33_spmd.clone.clone.clone, body=%wide.region_18.32_spmd.clone.clone.clone.sunk | while | flops 2336233984 | bytes 66357492 | solution.py:267
  322.6 2.0 collective-permute-start.1
  325.6 7.0 %collective-permute-done.1 = bf16[128,2048]{1,0:T(8,128)(2,1)S(1)} collective-permute-done((bf16[128,2048]{1,0:T(8,128)(2,1)}, bf16[128,2048]{1,0:T(8,128)(2,1)S(1)}, u32[]{:S(2)}, u32[]{:S(2)}) %collective-permute-start.1) | collective-permute-done | bytes 524320 | tf_op jit(solution)/shard_map/while/body/eval_jaxpr/ppermute | solution.py:263
  334.3 2.8 collective-permute-start.1
  338.1 10.3 %collective-permute-done.1 = bf16[128,2048]{1,0:T(8,128)(2,1)S(1)} collective-permute-done((bf16[128,2048]{1,0:T(8,128)(2,1)}, bf16[128,2048]{1,0:T(8,128)(2,1)S(1)}, u32[]{:S(2)}, u32[]{:S(2)}) %collective-permute-start.1) | collective-permute-done | bytes 524320 | tf_op jit(solution)/shard_map/while/body/eval_jaxpr/ppermute | solution.py:263
  350.1 2.0 collective-permute-start.1
  353.2 7.8 %collective-permute-done.1 = bf16[128,2048]{1,0:T(8,128)(2,1)S(1)} collective-permute-done((bf16[128,2048]{1,0:T(8,128)(2,1)}, bf16[128,2048]{1,0:T(8,128)(2,1)S(1)}, u32[]{:S(2)}, u32[]{:S(2)}) %collective-permute-start.1) | collective-permute-done | bytes 524320 | tf_op jit(solution)/shard_map/while/body/eval_jaxpr/ppermute | solution.py:263
  362.6 2.0 collective-permute-start.1
  365.7 7.8 %collective-permute-done.1 = bf16[128,2048]{1,0:T(8,128)(2,1)S(1)} collective-permute-done((bf16[128,2048]{1,0:T(8,128)(2,1)}, bf16[128,2048]{1,0:T(8,128)(2,1)S(1)}, u32[]{:S(2)}, u32[]{:S(2)}) %collective-permute-start.1) | collective-permute-done | bytes 524320 | tf_op jit(solution)/shard_map/while/body/eval_jaxpr/ppermute | solution.py:263
  375.1 2.0 collective-permute-start.1
  377.2 5.0 conditional.19
  377.4 4.7 fusion.69
  382.1 67.4 %collective-permute-done.1 = bf16[128,2048]{1,0:T(8,128)(2,1)S(1)} collective-permute-done((bf16[128,2048]{1,0:T(8,128)(2,1)}, bf16[128,2048]{1,0:T(8,128)(2,1)S(1)}, u32[]{:S(2)}, u32[]{:S(2)}) %collective-permute-start.1) | collective-permute-done | bytes 524320 | tf_op jit(solution)/shard_map/while/body/eval_jaxpr/ppermute | solution.py:263
  450.4 15.3 %conditional.18 = (bf16[128,2048]{1,0:T(8,128)(2,1)}, f32[2048]{0:T(1024)S(1)}) conditional(s32[]{:T(128)} %convert_element_type.349, () %tuple.188, (bf16[128,2048]{1,0:T(8,128)(2,1)S(1)}, bf16[1024,2048]{1,0:T(8,128)(2,1)}, s32[128]{0:T(128)S(1)}, f32[128,1536]{1,0:T(8,128)}, f32[128,1,32]{0,2,1:T(8,128)S(1)}, ...), branch_computations={%region_19.19_spmd, %region_20.28_spmd} | conditional | flops 1528560128 | bytes 55866488 | solution.py:260
  452.8 3.7 convolution_convert_fusion.4
  457.3 1.5 fusion.43
  458.8 1.4 fusion.51
  462.1 2.3 multiply_reduce_fusion.3
  465.6 2.0 collective-permute-start.1
  468.7 6.0 %collective-permute-done.1 = bf16[128,2048]{1,0:T(8,128)(2,1)S(1)} collective-permute-done((bf16[128,2048]{1,0:T(8,128)(2,1)}, bf16[128,2048]{1,0:T(8,128)(2,1)S(1)}, u32[]{:S(2)}, u32[]{:S(2)}) %collective-permute-start.1) | collective-permute-done | bytes 524320 | tf_op jit(solution)/shard_map/while/body/eval_jaxpr/ppermute | solution.py:263
  476.3 18.2 %collective-permute-start.1 = (bf16[128,2048]{1,0:T(8,128)(2,1)}, bf16[128,2048]{1,0:T(8,128)(2,1)S(1)}, u32[]{:S(2)}, u32[]{:S(2)}) collective-permute-start(bf16[128,2048]{1,0:T(8,128)(2,1)} %get-tuple-element.1275), channel_id=1, source_target_pairs={{32,0},{64,32},{96,64},{128,96},{160,128},{192,160},{224,192},{33,... | collective-permute-start | bytes 1572872 | tf_op jit(solution)/shard_map/while/body/eval_jaxpr/ppermute | solution.py:263
  495.5 6.0 %collective-permute-done.1 = bf16[128,2048]{1,0:T(8,128)(2,1)S(1)} collective-permute-done((bf16[128,2048]{1,0:T(8,128)(2,1)}, bf16[128,2048]{1,0:T(8,128)(2,1)S(1)}, u32[]{:S(2)}, u32[]{:S(2)}) %collective-permute-start.1) | collective-permute-done | bytes 524320 | tf_op jit(solution)/shard_map/while/body/eval_jaxpr/ppermute | solution.py:263
  503.2 3.8 collective-permute-start.1
  508.0 6.0 %collective-permute-done.1 = bf16[128,2048]{1,0:T(8,128)(2,1)S(1)} collective-permute-done((bf16[128,2048]{1,0:T(8,128)(2,1)}, bf16[128,2048]{1,0:T(8,128)(2,1)S(1)}, u32[]{:S(2)}, u32[]{:S(2)}) %collective-permute-start.1) | collective-permute-done | bytes 524320 | tf_op jit(solution)/shard_map/while/body/eval_jaxpr/ppermute | solution.py:263
  514.0 5.0 collective-permute-start.2
  519.0 2.5 collective-permute-start.4
  521.4 2.3 collective-permute-done.3
  525.5 1.5 collective-permute-start.5
  527.2 5.8 %collective-permute-start.7 = (f32[2048]{0:T(1024)S(1)}, f32[2048]{0:T(1024)S(1)}, u32[]{:S(2)}, u32[]{:S(2)}) collective-permute-start(f32[2048]{0:T(1024)S(1)} %bitcast.250), channel_id=1, source_target_pairs={{0,12},{1,13},{2,14},{3,15},{4,8},{5,9},{6,10},{7,11},{8,4},{9,5},... | collective-permute-start | bytes 24584 | tf_op jit(solution)/shard_map/ppermute | solution.py:128
  533.1 2.5 collective-permute-done.7
  535.7 2.8 collective-permute-start.8
  538.5 2.4 collective-permute-done.8
  (297 shorter events, 72.2 us)
Async XLA Ops:
  7.2 58.8 %copy-start.11 = (bf16[1,1024,64]{1,2,0:T(8,128)(2,1)S(1)}, bf16[1,1024,64]{1,2,0:T(8,128)(2,1)}, u32[]{:S(2)}) copy-start(bf16[1,1024,64]{1,2,0:T(8,128)(2,1)} %param.29) | copy-start | bytes 393220
  7.2 195.6 %all-gather.2.cloned.1.call-start = ((), (), s32[]{:S(2)}) async-start(), calls=%async_computation.2 | async-start | bytes 6488064 | tf_op jit(solution)/shard_map/all_gather | solution.py:179
  66.0 7.6 %copy-start.12 = (s32[4,32]{1,0:T(4,128)S(1)}, s32[4,32]{1,0:T(4,128)}, u32[]{:S(2)}) copy-start(s32[4,32]{1,0:T(4,128)} %param.23) | copy-start | bytes 1540
  68.6 127.7 %all-to-all-start.1 = ((bf16[32,1024,64]{1,2,0:T(8,128)(2,1)}), bf16[32,1024,64]{1,2,0:T(8,128)(2,1)}, u32[]{:S(2)}, u32[]{:S(2)}) async-start(bf16[32,1024,64]{1,2,0:T(8,128)(2,1)} %stack.62), calls=%async_computation.1 | async-start | bytes 8388608 | tf_op jit(solution)/shard_map/all_to_all | solution.py:184
  79.4 123.4 %copy-start.1 = (f32[1,2048]{1,0:T(1,128)S(1)}, f32[1,2048]{1,0:T(1,128)}, u32[]{:S(2)}) copy-start(f32[1,2048]{1,0:T(1,128)} %param.26) | copy-start | bytes 24580
  79.4 123.4 %copy-start.5 = (f32[1,2048]{1,0:T(1,128)S(1)}, f32[1,2048]{1,0:T(1,128)}, u32[]{:S(2)}) copy-start(f32[1,2048]{1,0:T(1,128)} %param.25) | copy-start | bytes 24580
  204.3 10.5 %collective-permute-start = (bf16[128,2048]{1,0:T(8,128)(2,1)S(1)}, bf16[128,2048]{1,0:T(8,128)(2,1)S(1)}, u32[]{:S(2)}, u32[]{:S(2)}) collective-permute-start(bf16[128,2048]{1,0:T(8,128)(2,1)S(1)} %get-tuple-element.1378), channel_id=1, source_target_pairs={{0,32},{32,64},{64,96},{96,128},{128,160},{160,192},{192,224},{1,3... | collective-permute-start | bytes 1572872 | tf_op jit(solution)/shard_map/while/body/eval_jaxpr/ppermute | solution.py:241
  216.3 19.8 %collective-permute-start = (bf16[128,2048]{1,0:T(8,128)(2,1)S(1)}, bf16[128,2048]{1,0:T(8,128)(2,1)S(1)}, u32[]{:S(2)}, u32[]{:S(2)}) collective-permute-start(bf16[128,2048]{1,0:T(8,128)(2,1)S(1)} %get-tuple-element.1378), channel_id=1, source_target_pairs={{0,32},{32,64},{64,96},{96,128},{128,160},{160,192},{192,224},{1,3... | collective-permute-start | bytes 1572872 | tf_op jit(solution)/shard_map/while/body/eval_jaxpr/ppermute | solution.py:241
  237.5 4.3 copy-start.2
  237.5 4.7 copy-start.8
  246.6 10.5 %collective-permute-start = (bf16[128,2048]{1,0:T(8,128)(2,1)S(1)}, bf16[128,2048]{1,0:T(8,128)(2,1)S(1)}, u32[]{:S(2)}, u32[]{:S(2)}) collective-permute-start(bf16[128,2048]{1,0:T(8,128)(2,1)S(1)} %get-tuple-element.1378), channel_id=1, source_target_pairs={{0,32},{32,64},{64,96},{96,128},{128,160},{160,192},{192,224},{1,3... | collective-permute-start | bytes 1572872 | tf_op jit(solution)/shard_map/while/body/eval_jaxpr/ppermute | solution.py:241
  258.6 10.5 %collective-permute-start = (bf16[128,2048]{1,0:T(8,128)(2,1)S(1)}, bf16[128,2048]{1,0:T(8,128)(2,1)S(1)}, u32[]{:S(2)}, u32[]{:S(2)}) collective-permute-start(bf16[128,2048]{1,0:T(8,128)(2,1)S(1)} %get-tuple-element.1378), channel_id=1, source_target_pairs={{0,32},{32,64},{64,96},{96,128},{128,160},{160,192},{192,224},{1,3... | collective-permute-start | bytes 1572872 | tf_op jit(solution)/shard_map/while/body/eval_jaxpr/ppermute | solution.py:241
  270.6 10.5 %collective-permute-start = (bf16[128,2048]{1,0:T(8,128)(2,1)S(1)}, bf16[128,2048]{1,0:T(8,128)(2,1)S(1)}, u32[]{:S(2)}, u32[]{:S(2)}) collective-permute-start(bf16[128,2048]{1,0:T(8,128)(2,1)S(1)} %get-tuple-element.1378), channel_id=1, source_target_pairs={{0,32},{32,64},{64,96},{96,128},{128,160},{160,192},{192,224},{1,3... | collective-permute-start | bytes 1572872 | tf_op jit(solution)/shard_map/while/body/eval_jaxpr/ppermute | solution.py:241
  282.7 13.1 %collective-permute-start = (bf16[128,2048]{1,0:T(8,128)(2,1)S(1)}, bf16[128,2048]{1,0:T(8,128)(2,1)S(1)}, u32[]{:S(2)}, u32[]{:S(2)}) collective-permute-start(bf16[128,2048]{1,0:T(8,128)(2,1)S(1)} %get-tuple-element.1378), channel_id=1, source_target_pairs={{0,32},{32,64},{64,96},{96,128},{128,160},{160,192},{192,224},{1,3... | collective-permute-start | bytes 1572872 | tf_op jit(solution)/shard_map/while/body/eval_jaxpr/ppermute | solution.py:241
  297.3 10.5 %collective-permute-start = (bf16[128,2048]{1,0:T(8,128)(2,1)S(1)}, bf16[128,2048]{1,0:T(8,128)(2,1)S(1)}, u32[]{:S(2)}, u32[]{:S(2)}) collective-permute-start(bf16[128,2048]{1,0:T(8,128)(2,1)S(1)} %get-tuple-element.1378), channel_id=1, source_target_pairs={{0,32},{32,64},{64,96},{96,128},{128,160},{160,192},{192,224},{1,3... | collective-permute-start | bytes 1572872 | tf_op jit(solution)/shard_map/while/body/eval_jaxpr/ppermute | solution.py:241
  309.3 10.5 %collective-permute-start = (bf16[128,2048]{1,0:T(8,128)(2,1)S(1)}, bf16[128,2048]{1,0:T(8,128)(2,1)S(1)}, u32[]{:S(2)}, u32[]{:S(2)}) collective-permute-start(bf16[128,2048]{1,0:T(8,128)(2,1)S(1)} %get-tuple-element.1378), channel_id=1, source_target_pairs={{0,32},{32,64},{64,96},{96,128},{128,160},{160,192},{192,224},{1,3... | collective-permute-start | bytes 1572872 | tf_op jit(solution)/shard_map/while/body/eval_jaxpr/ppermute | solution.py:241
  319.8 1.1 copy-start
  319.9 1.1 copy-start.9
  322.6 3.0 copy-start.6
  322.6 10.1 %copy-start.10 = (s32[128]{0:T(128)S(1)}, s32[128]{0:T(128)}, u32[]{:S(2)}) copy-start(s32[128]{0:T(128)} %get-tuple-element.1415) | copy-start | bytes 1540 | tf_op jit(solution)/shard_map/while
  322.6 10.0 %collective-permute-start.1 = (bf16[128,2048]{1,0:T(8,128)(2,1)}, bf16[128,2048]{1,0:T(8,128)(2,1)S(1)}, u32[]{:S(2)}, u32[]{:S(2)}) collective-permute-start(bf16[128,2048]{1,0:T(8,128)(2,1)} %get-tuple-element.1275), channel_id=1, source_target_pairs={{32,0},{64,32},{96,64},{128,96},{160,128},{192,160},{224,192},{33,... | collective-permute-start | bytes 1572872 | tf_op jit(solution)/shard_map/while/body/eval_jaxpr/ppermute | solution.py:263
  325.6 7.0 %copy-start.7 = (f32[2048]{0:T(1024)}, f32[2048]{0:T(1024)S(1)}, u32[]{:S(2)}) copy-start(f32[2048]{0:T(1024)S(1)} %select_add_fusion.2) | copy-start | bytes 24580 | tf_op jit(solution)/shard_map/while
  334.3 3.8 copy-start.6
  334.3 14.2 %copy-start.10 = (s32[128]{0:T(128)S(1)}, s32[128]{0:T(128)}, u32[]{:S(2)}) copy-start(s32[128]{0:T(128)} %get-tuple-element.1415) | copy-start | bytes 1540 | tf_op jit(solution)/shard_map/while
  334.3 14.2 %collective-permute-start.1 = (bf16[128,2048]{1,0:T(8,128)(2,1)}, bf16[128,2048]{1,0:T(8,128)(2,1)S(1)}, u32[]{:S(2)}, u32[]{:S(2)}) collective-permute-start(bf16[128,2048]{1,0:T(8,128)(2,1)} %get-tuple-element.1275), channel_id=1, source_target_pairs={{32,0},{64,32},{96,64},{128,96},{160,128},{192,160},{224,192},{33,... | collective-permute-start | bytes 1572872 | tf_op jit(solution)/shard_map/while/body/eval_jaxpr/ppermute | solution.py:263
  338.1 10.3 %copy-start.7 = (f32[2048]{0:T(1024)}, f32[2048]{0:T(1024)S(1)}, u32[]{:S(2)}) copy-start(f32[2048]{0:T(1024)S(1)} %select_add_fusion.2) | copy-start | bytes 24580 | tf_op jit(solution)/shard_map/while
  350.1 3.0 copy-start.6
  350.1 10.8 %copy-start.10 = (s32[128]{0:T(128)S(1)}, s32[128]{0:T(128)}, u32[]{:S(2)}) copy-start(s32[128]{0:T(128)} %get-tuple-element.1415) | copy-start | bytes 1540 | tf_op jit(solution)/shard_map/while
  350.1 10.8 %collective-permute-start.1 = (bf16[128,2048]{1,0:T(8,128)(2,1)}, bf16[128,2048]{1,0:T(8,128)(2,1)S(1)}, u32[]{:S(2)}, u32[]{:S(2)}) collective-permute-start(bf16[128,2048]{1,0:T(8,128)(2,1)} %get-tuple-element.1275), channel_id=1, source_target_pairs={{32,0},{64,32},{96,64},{128,96},{160,128},{192,160},{224,192},{33,... | collective-permute-start | bytes 1572872 | tf_op jit(solution)/shard_map/while/body/eval_jaxpr/ppermute | solution.py:263
  353.2 7.8 %copy-start.7 = (f32[2048]{0:T(1024)}, f32[2048]{0:T(1024)S(1)}, u32[]{:S(2)}) copy-start(f32[2048]{0:T(1024)S(1)} %select_add_fusion.2) | copy-start | bytes 24580 | tf_op jit(solution)/shard_map/while
  362.6 3.0 copy-start.6
  362.6 10.8 %copy-start.10 = (s32[128]{0:T(128)S(1)}, s32[128]{0:T(128)}, u32[]{:S(2)}) copy-start(s32[128]{0:T(128)} %get-tuple-element.1415) | copy-start | bytes 1540 | tf_op jit(solution)/shard_map/while
  362.6 10.8 %collective-permute-start.1 = (bf16[128,2048]{1,0:T(8,128)(2,1)}, bf16[128,2048]{1,0:T(8,128)(2,1)S(1)}, u32[]{:S(2)}, u32[]{:S(2)}) collective-permute-start(bf16[128,2048]{1,0:T(8,128)(2,1)} %get-tuple-element.1275), channel_id=1, source_target_pairs={{32,0},{64,32},{96,64},{128,96},{160,128},{192,160},{224,192},{33,... | collective-permute-start | bytes 1572872 | tf_op jit(solution)/shard_map/while/body/eval_jaxpr/ppermute | solution.py:263
  365.7 7.8 %copy-start.7 = (f32[2048]{0:T(1024)}, f32[2048]{0:T(1024)S(1)}, u32[]{:S(2)}) copy-start(f32[2048]{0:T(1024)S(1)} %select_add_fusion.2) | copy-start | bytes 24580 | tf_op jit(solution)/shard_map/while
  375.1 7.0 %copy-start.6 = (f32[2048]{0:T(1024)S(1)}, f32[2048]{0:T(1024)}, u32[]{:S(2)}) copy-start(f32[2048]{0:T(1024)} %get-tuple-element.1343) | copy-start | bytes 24580 | tf_op jit(solution)/shard_map/while
  375.1 74.5 %copy-start.10 = (s32[128]{0:T(128)S(1)}, s32[128]{0:T(128)}, u32[]{:S(2)}) copy-start(s32[128]{0:T(128)} %get-tuple-element.1415) | copy-start | bytes 1540 | tf_op jit(solution)/shard_map/while
  375.1 74.5 %collective-permute-start.1 = (bf16[128,2048]{1,0:T(8,128)(2,1)}, bf16[128,2048]{1,0:T(8,128)(2,1)S(1)}, u32[]{:S(2)}, u32[]{:S(2)}) collective-permute-start(bf16[128,2048]{1,0:T(8,128)(2,1)} %get-tuple-element.1275), channel_id=1, source_target_pairs={{32,0},{64,32},{96,64},{128,96},{160,128},{192,160},{224,192},{33,... | collective-permute-start | bytes 1572872 | tf_op jit(solution)/shard_map/while/body/eval_jaxpr/ppermute | solution.py:263
  382.1 67.5 %copy-start.7 = (f32[2048]{0:T(1024)}, f32[2048]{0:T(1024)S(1)}, u32[]{:S(2)}) copy-start(f32[2048]{0:T(1024)S(1)} %select_add_fusion.2) | copy-start | bytes 24580 | tf_op jit(solution)/shard_map/while
  452.0 0.7 copy-start.3
  456.5 4.9 copy-start.4
  457.3 4.8 slice-start
  460.3 1.9 slice-start.1
  465.6 3.0 copy-start.6
  465.6 9.0 %copy-start.10 = (s32[128]{0:T(128)S(1)}, s32[128]{0:T(128)}, u32[]{:S(2)}) copy-start(s32[128]{0:T(128)} %get-tuple-element.1415) | copy-start | bytes 1540 | tf_op jit(solution)/shard_map/while
  465.6 9.0 %collective-permute-start.1 = (bf16[128,2048]{1,0:T(8,128)(2,1)}, bf16[128,2048]{1,0:T(8,128)(2,1)S(1)}, u32[]{:S(2)}, u32[]{:S(2)}) collective-permute-start(bf16[128,2048]{1,0:T(8,128)(2,1)} %get-tuple-element.1275), channel_id=1, source_target_pairs={{32,0},{64,32},{96,64},{128,96},{160,128},{192,160},{224,192},{33,... | collective-permute-start | bytes 1572872 | tf_op jit(solution)/shard_map/while/body/eval_jaxpr/ppermute | solution.py:263
  468.7 6.0 %copy-start.7 = (f32[2048]{0:T(1024)}, f32[2048]{0:T(1024)S(1)}, u32[]{:S(2)}) copy-start(f32[2048]{0:T(1024)S(1)} %select_add_fusion.2) | copy-start | bytes 24580 | tf_op jit(solution)/shard_map/while
  476.3 19.2 %copy-start.6 = (f32[2048]{0:T(1024)S(1)}, f32[2048]{0:T(1024)}, u32[]{:S(2)}) copy-start(f32[2048]{0:T(1024)} %get-tuple-element.1343) | copy-start | bytes 24580 | tf_op jit(solution)/shard_map/while
  476.3 25.2 %copy-start.10 = (s32[128]{0:T(128)S(1)}, s32[128]{0:T(128)}, u32[]{:S(2)}) copy-start(s32[128]{0:T(128)} %get-tuple-element.1415) | copy-start | bytes 1540 | tf_op jit(solution)/shard_map/while
  476.3 25.2 %collective-permute-start.1 = (bf16[128,2048]{1,0:T(8,128)(2,1)}, bf16[128,2048]{1,0:T(8,128)(2,1)S(1)}, u32[]{:S(2)}, u32[]{:S(2)}) collective-permute-start(bf16[128,2048]{1,0:T(8,128)(2,1)} %get-tuple-element.1275), channel_id=1, source_target_pairs={{32,0},{64,32},{96,64},{128,96},{160,128},{192,160},{224,192},{33,... | collective-permute-start | bytes 1572872 | tf_op jit(solution)/shard_map/while/body/eval_jaxpr/ppermute | solution.py:263
  495.5 6.0 %copy-start.7 = (f32[2048]{0:T(1024)}, f32[2048]{0:T(1024)S(1)}, u32[]{:S(2)}) copy-start(f32[2048]{0:T(1024)S(1)} %select_add_fusion.2) | copy-start | bytes 24580 | tf_op jit(solution)/shard_map/while
  503.2 4.8 copy-start.6
  503.2 10.8 %copy-start.10 = (s32[128]{0:T(128)S(1)}, s32[128]{0:T(128)}, u32[]{:S(2)}) copy-start(s32[128]{0:T(128)} %get-tuple-element.1415) | copy-start | bytes 1540 | tf_op jit(solution)/shard_map/while
  503.2 10.8 %collective-permute-start.1 = (bf16[128,2048]{1,0:T(8,128)(2,1)}, bf16[128,2048]{1,0:T(8,128)(2,1)S(1)}, u32[]{:S(2)}, u32[]{:S(2)}) collective-permute-start(bf16[128,2048]{1,0:T(8,128)(2,1)} %get-tuple-element.1275), channel_id=1, source_target_pairs={{32,0},{64,32},{96,64},{128,96},{160,128},{192,160},{224,192},{33,... | collective-permute-start | bytes 1572872 | tf_op jit(solution)/shard_map/while/body/eval_jaxpr/ppermute | solution.py:263
  508.0 6.0 %copy-start.7 = (f32[2048]{0:T(1024)}, f32[2048]{0:T(1024)S(1)}, u32[]{:S(2)}) copy-start(f32[2048]{0:T(1024)S(1)} %select_add_fusion.2) | copy-start | bytes 24580 | tf_op jit(solution)/shard_map/while
  514.0 7.4 %collective-permute-start.2 = (f32[2048]{0:T(1024)}, f32[2048]{0:T(1024)S(1)}, u32[]{:S(2)}, u32[]{:S(2)}) collective-permute-start(f32[2048]{0:T(1024)} %get-tuple-element.1399), channel_id=1, source_target_pairs={{0,1},{1,0},{2,3},{3,2},{4,5},{5,4},{6,7},{7,6},{8,9},{9,8},{10,11... | collective-permute-start | bytes 24584 | tf_op jit(solution)/shard_map/ppermute | solution.py:128
  519.0 4.8 collective-permute-start.3
  519.0 5.7 %collective-permute-start.4 = (f32[2048]{0:T(1024)}, f32[2048]{0:T(1024)S(1)}, u32[]{:S(2)}, u32[]{:S(2)}) collective-permute-start(f32[2048]{0:T(1024)} %get-tuple-element.1399), channel_id=1, source_target_pairs={{0,3},{1,2},{2,1},{3,0},{4,7},{5,6},{6,5},{7,4},{8,11},{9,10},{10,... | collective-permute-start | bytes 24584 | tf_op jit(solution)/shard_map/ppermute | solution.py:128
  525.5 7.6 %collective-permute-start.5 = (f32[2048]{0:T(1024)S(1)}, f32[2048]{0:T(1024)S(1)}, u32[]{:S(2)}, u32[]{:S(2)}) collective-permute-start(f32[2048]{0:T(1024)S(1)} %bitcast.248), channel_id=1, source_target_pairs={{0,4},{1,5},{2,6},{3,7},{4,0},{5,1},{6,2},{7,3},{8,12},{9,13},{10,... | collective-permute-start | bytes 24584 | tf_op jit(solution)/shard_map/ppermute | solution.py:128
  526.9 6.2 %collective-permute-start.6 = (f32[2048]{0:T(1024)S(1)}, f32[2048]{0:T(1024)S(1)}, u32[]{:S(2)}, u32[]{:S(2)}) collective-permute-start(f32[2048]{0:T(1024)S(1)} %bitcast.249), channel_id=1, source_target_pairs={{0,8},{1,9},{2,10},{3,11},{4,12},{5,13},{6,14},{7,15},{8,0},{9,1},... | collective-permute-start | bytes 24584 | tf_op jit(solution)/shard_map/ppermute | solution.py:128
  527.2 8.5 %collective-permute-start.7 = (f32[2048]{0:T(1024)S(1)}, f32[2048]{0:T(1024)S(1)}, u32[]{:S(2)}, u32[]{:S(2)}) collective-permute-start(f32[2048]{0:T(1024)S(1)} %bitcast.250), channel_id=1, source_target_pairs={{0,12},{1,13},{2,14},{3,15},{4,8},{5,9},{6,10},{7,11},{8,4},{9,5},... | collective-permute-start | bytes 24584 | tf_op jit(solution)/shard_map/ppermute | solution.py:128
  535.7 5.2 collective-permute-start.8
Sparse Core Ops, SparseCore 0:
  10.6 163.5 all-gather.1
